TPU v7x, 256 devices: a whole 4x4x8 slice. The times are simulated.
256 devices in a mesh: dp: 2 (over y_hi), ctx: 64 (over y_lo, x, z), head: 2 (over core).
Axes of the slice: x: 4, y: 4 (y_hi: 2, y_lo: 2; y = y_hi * 2 + y_lo), z: 8, core: 2. Of those that a mesh axis runs over, the one named last changes fastest.
Arguments:
- hidden_in: bfloat16 [2, 8192, 4096], P('dp', 'ctx'), may hold values from -16 to 16
- proj_weight: bfloat16 [4096, 2, 256], P(('dp', 'ctx'), None, 'head'), may hold values from -0.0029296875 to 0.0029296875
- values_in: bfloat16 [2, 8192, 4096], P('dp', 'ctx', 'head'), may hold values from -6 to 6
- gate_in: bfloat16 [2, 8192, 4096], P('dp', 'ctx', 'head'), may hold values from -6 to 6
- log_decay: float32 [2, 64, 8192], P('dp', 'head', 'ctx'), may hold values from -1 to 0, as said below
- skip_gain: float32 [64], P('head'), may hold values from 0.5 to 2
- grad_out: bfloat16 [2, 8192, 4096], P('dp', 'ctx', 'head'), may hold values from -6 to 6
Outputs:
- grad_input: bfloat16 [2, 8192, 4096], P('dp', 'ctx', 'head')
- grad_values: bfloat16 [2, 8192, 4096], P('dp', 'ctx', 'head')
- grad_gate: bfloat16 [2, 8192, 4096], P('dp', 'ctx', 'head')
- grad_proj: float32 [4096, 2, 256], P(('dp', 'ctx'), None, 'head')
Inputs may be any that keep to these rules, and one draw needn't show every extreme that they name: `log_decay`: logarithms of the per-token decay of each head's state; all values are at most zero.
All inputs are finite; a program needn't handle non-finite values.
Results may differ from a plain program's by a relative error of at most 0.011.
Values may be sent and summed in bfloat16 or wider, within the bound.
No kernel may reach another device: no remote copies, remote signals or barrier semaphores. Data moves between devices by JAX's collectives and lax.ppermute only.
A program may use at most 192 MiB of HBM per device.

v0:
```python
import jax
import jax.numpy as jnp
from jax import lax
from jax.sharding import PartitionSpec as P

HEAD_DIM = 64
STATE = 64
SPAN = 128


def carried_in(part, axis, combine, identity, reverse):
    count = lax.axis_size(axis)
    place = lax.axis_index(axis)
    ahead = count - 1 - place if reverse else place
    gathered = jax.tree.map(lambda a: lax.all_gather(a, axis), part)
    state = jax.tree.map(lambda a, e: jnp.zeros_like(a) + jnp.asarray(e, a.dtype), part, identity)

    def one(lap, state):
        source = count - 1 - lap if reverse else lap
        return combine(
            state, jax.tree.map(lambda a: lax.dynamic_index_in_dim(a, source, 0, False), gathered)
        )

    return lax.fori_loop(0, ahead, one, state)


def span_summary(b_vals, c_vals, x_vals, dy_round, rate_vals):
    block_len = x_vals.shape[0]
    head_count = x_vals.shape[1]
    group_count = b_vals.shape[1]
    per_group = head_count // group_count
    cumlog = jnp.cumsum(rate_vals, axis=1)
    final_log = cumlog[:, -1]
    to_end = jnp.exp(final_log[:, None] - cumlog)
    from_start = jnp.exp(cumlog)
    b_wide = b_vals.astype(jnp.float32)
    c_wide = c_vals.astype(jnp.float32)
    x_scaled = (x_vals.astype(jnp.float32) * to_end.T[:, :, None]).reshape(
        block_len, group_count, per_group, HEAD_DIM
    )
    dy_scaled = (dy_round.astype(jnp.float32) * from_start.T[:, :, None]).reshape(
        block_len, group_count, per_group, HEAD_DIM
    )
    state_part = jnp.einsum("qgn,qgkp->ngkp", b_wide, x_scaled, precision=lax.Precision.HIGHEST)
    adjoint_part = jnp.einsum("qgn,qgkp->ngkp", c_wide, dy_scaled, precision=lax.Precision.HIGHEST)
    return (jnp.exp(final_log), state_part.reshape(STATE, -1), adjoint_part.reshape(STATE, -1))


def span_full(
    b_vals,
    c_vals,
    x_vals,
    dy_round,
    rate_vals,
    skip_vals,
    state_in,
    adjoint_out,
    dout_vals,
    gate_vals,
):
    block_len = x_vals.shape[0]
    head_count = x_vals.shape[1]
    group_count = b_vals.shape[1]
    per_group = head_count // group_count
    cumlog = jnp.cumsum(rate_vals, axis=1)
    final_log = cumlog[:, -1]
    to_end = jnp.exp(final_log[:, None] - cumlog)
    from_start = jnp.exp(cumlog)
    causal = jnp.arange(block_len)[:, None] >= jnp.arange(block_len)[None, :]
    log_gaps = cumlog[:, :, None] - cumlog[:, None, :]
    decays = jnp.where(causal[None], jnp.exp(jnp.where(causal[None], log_gaps, 0.0)), 0.0)
    b_wide = b_vals.astype(jnp.float32)
    c_wide = c_vals.astype(jnp.float32)
    cb_dots = jnp.einsum("tgn,sgn->gts", c_vals, b_vals, preferred_element_type=jnp.float32)
    mixer_bf = (decays * jnp.repeat(cb_dots, per_group, axis=0)).astype(jnp.bfloat16)
    state_four = state_in.reshape(STATE, group_count, per_group, HEAD_DIM)
    adjoint_four = adjoint_out.reshape(STATE, group_count, per_group, HEAD_DIM)
    y_intra = jnp.einsum("hts,shp->thp", mixer_bf, x_vals, preferred_element_type=jnp.float32)
    y_inter = jnp.einsum(
        "tgn,ngkp->tgkp", c_wide, state_four, precision=lax.Precision.HIGHEST
    ).reshape(block_len, head_count, HEAD_DIM)
    x_wide = x_vals.astype(jnp.float32)
    output_pre = y_intra + y_inter * from_start.T[:, :, None] + skip_vals[None, :, None] * x_wide
    gate_wide = gate_vals.astype(jnp.float32)
    gate_sig = jax.nn.sigmoid(gate_wide)
    grad_gate = (
        dout_vals.astype(jnp.float32) * output_pre * gate_sig * (1.0 + gate_wide * (1.0 - gate_sig))
    ).astype(jnp.bfloat16)
    dy_wide = dy_round.astype(jnp.float32)
    x_inter = jnp.einsum(
        "sgn,ngkp->sgkp", b_wide, adjoint_four, precision=lax.Precision.HIGHEST
    ).reshape(block_len, head_count, HEAD_DIM)
    grad_vals = (
        jnp.einsum("hts,thp->shp", mixer_bf, dy_round, preferred_element_type=jnp.float32)
        + x_inter * to_end.T[:, :, None]
        + skip_vals[None, :, None] * dy_wide
    )
    mix_grad = (
        jnp.einsum("thp,shp->hts", dy_round, x_vals, preferred_element_type=jnp.float32) * decays
    )
    dots_grad = (
        mix_grad.reshape(group_count, per_group, block_len, block_len)
        .sum(axis=1)
        .astype(jnp.bfloat16)
    )
    dy_scaled = (dy_wide * from_start.T[:, :, None]).reshape(
        block_len, group_count, per_group, HEAD_DIM
    )
    x_scaled = (x_wide * to_end.T[:, :, None]).reshape(block_len, group_count, per_group, HEAD_DIM)
    c_grad = jnp.einsum(
        "gts,sgn->tgn", dots_grad, b_vals, preferred_element_type=jnp.float32
    ) + jnp.einsum("tgkp,ngkp->tgn", dy_scaled, state_four, precision=lax.Precision.HIGHEST)
    b_grad = jnp.einsum(
        "gts,tgn->sgn", dots_grad, c_vals, preferred_element_type=jnp.float32
    ) + jnp.einsum("sgkp,ngkp->sgn", x_scaled, adjoint_four, precision=lax.Precision.HIGHEST)
    return (grad_vals.astype(jnp.bfloat16), grad_gate, jnp.stack([b_grad, c_grad], axis=1))


def chain(earlier, later):
    return (earlier[0] * later[0], earlier[1] * jnp.repeat(later[0], HEAD_DIM)[None, :] + later[1])


def body(hidden_in, proj_weight, values_in, gate_in, log_decay, skip_gain, grad_out):
    tokens = hidden_in[0]
    tok_rows = tokens.shape[0]
    weight_local = proj_weight.reshape(proj_weight.shape[0], -1)
    col_count = weight_local.shape[1]
    weight_full = lax.all_gather(weight_local, ("dp", "ctx"), axis=0, tiled=True)
    bc_sums = jnp.dot(tokens, weight_full, preferred_element_type=jnp.float32)
    group_count = col_count // (2 * STATE)
    head_count = values_in.shape[2] // HEAD_DIM
    nblocks = tok_rows // SPAN
    bc_vals = bc_sums.astype(jnp.bfloat16).reshape(nblocks, SPAN, 2, group_count, STATE)
    x_vals = values_in[0].reshape(nblocks, SPAN, head_count, HEAD_DIM)
    gate_vals = gate_in[0].reshape(nblocks, SPAN, head_count, HEAD_DIM)
    dout_vals = grad_out[0].reshape(nblocks, SPAN, head_count, HEAD_DIM)
    dy_round = (dout_vals.astype(jnp.float32) * jax.nn.silu(gate_vals.astype(jnp.float32))).astype(
        jnp.bfloat16
    )
    rate_vals = log_decay[0].reshape(head_count, nblocks, SPAN)
    summaries = [
        span_summary(bc_vals[0, :, 0], bc_vals[0, :, 1], x_vals[0], dy_round[0], rate_vals[:, 0])
    ]
    dev_decay = jnp.ones((head_count,), jnp.float32)
    dev_state = jnp.zeros((STATE, head_count * HEAD_DIM), jnp.float32)
    dev_adjoint = jnp.zeros((STATE, head_count * HEAD_DIM), jnp.float32)
    block_id = 0
    dev_state = (
        dev_state * jnp.repeat(summaries[block_id][0], HEAD_DIM)[None, :] + summaries[block_id][1]
    )
    dev_decay = dev_decay * summaries[block_id][0]
    for block_id in reversed(range(nblocks)):
        dev_adjoint = (
            dev_adjoint * jnp.repeat(summaries[block_id][0], HEAD_DIM)[None, :]
            + summaries[block_id][2]
        )
    identity = (
        jnp.ones((head_count,), jnp.float32),
        jnp.zeros((STATE, head_count * HEAD_DIM), jnp.float32),
    )
    state_start = carried_in((dev_decay, dev_state), "ctx", chain, identity, False)[1]
    adjoint_end = carried_in((dev_decay, dev_adjoint), "ctx", chain, identity, True)[1]
    running = state_start
    block_id = 0
    states_in = running
    adjoints_out = [None] * nblocks
    running = adjoint_end
    for block_id in reversed(range(nblocks)):
        adjoints_out[block_id] = running
        running = (
            running * jnp.repeat(summaries[block_id][0], HEAD_DIM)[None, :] + summaries[block_id][2]
        )
    results = [
        span_full(
            bc_vals[0, :, 0],
            bc_vals[0, :, 1],
            x_vals[0],
            dy_round[0],
            rate_vals[:, 0],
            skip_gain,
            states_in,
            adjoints_out[0],
            dout_vals[0],
            gate_vals[0],
        )
    ]
    grad_values = jnp.concatenate([entry[0] for entry in results], axis=0).reshape(
        1, tok_rows, head_count * HEAD_DIM
    )
    grad_gate = jnp.concatenate([entry[1] for entry in results], axis=0).reshape(
        1, tok_rows, head_count * HEAD_DIM
    )
    grad_flat = (
        jnp.concatenate([entry[2] for entry in results], axis=0)
        .reshape(tok_rows, col_count)
        .astype(jnp.bfloat16)
    )
    input_terms = jnp.einsum(
        "tc,dc->td", grad_flat, weight_full, preferred_element_type=jnp.float32
    )
    grad_input = lax.psum_scatter(
        input_terms.astype(jnp.bfloat16), "head", scatter_dimension=1, tiled=True
    )[None]
    scale = 1.0 / (lax.axis_size("dp") * lax.axis_size("ctx") * tok_rows)
    grad_proj = lax.psum_scatter(
        jnp.einsum("td,tc->dc", tokens, grad_flat, preferred_element_type=jnp.float32) * scale,
        ("dp", "ctx"),
        scatter_dimension=0,
        tiled=True,
    )
    grad_proj = grad_proj.reshape(-1, 2, col_count // 2)
    return (grad_input, grad_values, grad_gate, grad_proj)


def solution(mesh):
    return jax.shard_map(
        body,
        mesh=mesh,
        in_specs=(
            P("dp", "ctx", None),
            P(("dp", "ctx"), None, "head"),
            P("dp", "ctx", "head"),
            P("dp", "ctx", "head"),
            P("dp", "head", "ctx"),
            P("head"),
            P("dp", "ctx", "head"),
        ),
        out_specs=(
            P("dp", "ctx", "head"),
            P("dp", "ctx", "head"),
            P("dp", "ctx", "head"),
            P(("dp", "ctx"), None, "head"),
        ),
        check_vma=False,
    )
```

profile of v0, /device:TPU:1, one launch (start us, length us, event | category | flops | bytes accessed | tf_op | source)
XLA Modules:
  0.0 1724.1 jit_solution(12229518481348502227)
XLA Ops:
  7.2 1.4 copy.67
  8.8 1.3 copy.44
  12.9 2.0 copy.46
  16.2 109.6 %all-gather.5.cloned.1.call-done = bf16[4096,256]{1,0:T(8,128)(2,1)} async-done(((bf16[32,256]{1,0:T(8,128)(2,1)}), bf16[4096,256]{1,0:T(8,128)(2,1)}) %all-gather.5.cloned.1.call-update) | async-done | bytes 2097168 | tf_op jit(solution)/shard_map/all_gather | solution.py:128
  125.8 2.0 convolution_convert_fusion.1
  127.9 2.7 fusion.17
  130.6 2.3 copy.47
  132.9 2.7 fusion.14
  135.6 2.4 copy.50
  137.9 2.3 broadcast_add_fusion.1
  142.4 147.3 %all-reduce = f32[2048]{0:T(1024)S(1)} all-reduce(f32[2048]{0:T(1024)S(1)} %dynamic-update-slice), channel_id=2, replica_groups=mesh['dp'=2,'ctx'=64,'head'=2] {'ctx'}, use_global_device_ids=true, to_apply=%add | all-reduce | flops 2048 | bytes 16384
  292.0 227.4 %all-gather.9.cloned.1.call-done = f32[64,64,2048]{2,1,0:T(8,128)} async-done(((f32[1,64,2048]{2,1,0:T(8,128)}), f32[64,64,2048]{2,1,0:T(8,128)}) %all-gather.9.cloned.1.call-update) | async-done | bytes 33554448 | tf_op jit(solution)/shard_map/all_gather | solution.py:15
  519.5 1.3 copy.64
  520.9 3.1 convolution_bitcast_fusion.2
  523.9 370.8 %all-gather.7.cloned.1.call-done = f32[64,64,2048]{2,1,0:T(8,128)} async-done(((f32[1,64,2048]{2,1,0:T(8,128)}), f32[64,64,2048]{2,1,0:T(8,128)}) %all-gather.7.cloned.1.call-update) | async-done | bytes 33554448 | tf_op jit(solution)/shard_map/all_gather | solution.py:15
  894.8 90.5 %while.26 = (s32[]{:T(128)}, f32[64,2048]{1,0:T(8,128)S(1)}, s32[]{:T(128)}, f32[64,32]{1,0:T(8,128)S(1)}, f32[64,64,2048]{2,1,0:T(8,128)}, /*index=5*/s32[]{:T(128)}, s32[]{:T(128)}, s32[]{:T(128)}, s32[]{:T(128)}) while((s32[]{:T(128)}, f32[64,2048]{1,0:T(8,128)S(1)}, s32[]{:T(128)}, f32[64,32]{1,0:T(8,128)S(1)}, f32[64,64,2048]{2,1,0:T(8,128)}, ...), condition=%wide.region_3.4_spmd, body=%wide.region_2.3_spmd.sunk | while | flops 262150 | bytes 1606171 | solution.py:24
  985.3 1.4 copy.63
  986.7 3.1 convolution_bitcast_fusion.3
  990.1 2.7 fusion
  992.8 5.6 copy.61
  998.7 3.5 convolution_convert_fusion
  1005.8 2.0 copy.54
  1011.3 590.0 %reduce-scatter.7.cloned.1.call-done = f32[32,256]{1,0:T(8,128)} async-done(((f32[4096,256]{1,0:T(8,128)}), f32[32,256]{1,0:T(8,128)}) %reduce-scatter.7.cloned.1.call-update) | async-done | bytes 32784
  1602.9 114.7 %reduce-scatter.5.cloned.1.call-done = bf16[128,2048]{1,0:T(8,128)(2,1)} async-done(((bf16[128,4096]{1,0:T(8,128)(2,1)}), bf16[128,2048]{1,0:T(8,128)(2,1)}) %reduce-scatter.5.cloned.1.call-update) | async-done | bytes 524304 | tf_op jit(solution)/shard_map/reduce_scatter | solution.py:201
  (331 shorter events, 105.8 us)
Async XLA Ops:
  7.2 118.6 %copy-start = (bf16[1,128,4096]{2,1,0:T(8,128)(2,1)S(1)}, bf16[1,128,4096]{2,1,0:T(8,128)(2,1)}, u32[]{:S(2)}) copy-start(bf16[1,128,4096]{2,1,0:T(8,128)(2,1)} %param.11) | copy-start | bytes 3145732
  7.2 3.0 copy-start.13
  7.2 118.6 %all-gather.5.cloned.1.call-start = ((), (), s32[]{:S(2)}) async-start(), calls=%async_computation.2 | async-start | bytes 2113536 | tf_op jit(solution)/shard_map/all_gather | solution.py:128
  8.7 510.7 %all-gather.9.cloned.1.call-start = ((), (), s32[]{:S(2)}) async-start(), calls=%async_computation.4 | async-start | bytes 34078720 | tf_op jit(solution)/shard_map/all_gather | solution.py:15
  10.1 2.2 copy-start.14
  12.3 277.5 %copy-start.2 = (f32[1,128,2048]{1,2,0:T(8,128)}, f32[1,128,2048]{1,2,0:T(8,128)S(1)}, u32[]{:S(2)}) copy-start(f32[1,128,2048]{1,2,0:T(8,128)S(1)} %convert_element_type.117) | copy-start | bytes 3145732
  135.6 5.4 copy-start.16
  140.2 754.5 %all-gather.7.cloned.1.call-start = ((), (), s32[]{:S(2)}) async-start(), calls=%async_computation.3 | async-start | bytes 34078720 | tf_op jit(solution)/shard_map/all_gather | solution.py:15
  141.0 1460.4 %reduce-scatter.7.cloned.1.call-start = ((), (), s32[]{:S(2)}) async-start(), calls=%async_computation.6 | async-start | bytes 4227072
  289.8 1.1 copy-start.7
  290.1 0.8 copy-start.11
  519.5 1.4 copy-start.6
  894.8 92.0 %copy-start.8 = (bf16[1,128,2048]{1,2,0:T(8,128)(2,1)S(1)}, bf16[1,128,2048]{1,2,0:T(8,128)(2,1)}, u32[]{:S(2)}) copy-start(bf16[1,128,2048]{1,2,0:T(8,128)(2,1)} %copy.46) | copy-start | bytes 1572868
  998.5 4.7 copy-start.5
  998.5 719.1 %reduce-scatter.5.cloned.1.call-start = ((), (), s32[]{:S(2)}) async-start(), calls=%async_computation.5 | async-start | bytes 1572864 | tf_op jit(solution)/shard_map/reduce_scatter | solution.py:201
  1003.2 1.0 copy-start.9
  1003.2 1.4 copy-start.12
  1003.2 1.4 copy-start.15
  1004.6 3.3 copy-start.4
  1007.8 1.2 copy-start.3
  1007.8 1.5 copy-start.10
  1009.4 708.2 %copy-start.1 = (bf16[1,128,4096]{2,1,0:T(8,128)(2,1)S(1)}, bf16[1,128,4096]{2,1,0:T(8,128)(2,1)}, u32[]{:S(2)}) copy-start(bf16[1,128,4096]{2,1,0:T(8,128)(2,1)} %param.11) | copy-start | bytes 3145732
Sparse Core Ops, SparseCore 0:
  12.2 113.5 all-gather.4
  140.3 379.0 all-gather.8
  521.8 372.8 all-gather.6
  998.6 602.7 reduce-scatter.6
  1604.3 113.2 reduce-scatter.4
where the time goes:
time: 1730 us; the launch traced here: 1720 us
  waiting for transfers between devices  1410 us (82%)
  blocking collectives  147 us (8%)
  other arithmetic  85.1 us (5%)
  local copies, waits for them, and re-layouts  36.8 us (2%)
  matrix products  24.6 us (1%)
    all_gather x2, waiting for transfers between devices, carried_in(): gathered = jax.tree.map(lambda a: lax.all_gather(a, axis), part)  598 us
    unnamed x6, waiting for transfers between devices  591 us
    unnamed x1, blocking collectives  147 us
    reduce_scatter x1, waiting for transfers between devices, body(): lax.psum_scatter(input_terms.astype(jnp.bfloat16), 'head', scatter_dimens...  115 us
    all_gather x1, waiting for transfers between devices, body(): lax.all_gather(weight_local, ('dp', 'ctx'), axis=0, tiled=True)  110 us
    add x63, other arithmetic, chain(): earlier[1] * jnp.repeat(later[0], HEAD_DIM)[None, :] + later[1]  78.9 us
  transfers between devices with their start and end apart: 5, of which 5 were waited for; matrix products, arithmetic and copies ran while one was open for 2% of the time, Pallas kernels for 0%

commit v1 on v0

--- a/solution.py
+++ b/solution.py
@@ -125,7 +125,12 @@
     tok_rows = tokens.shape[0]
     weight_local = proj_weight.reshape(proj_weight.shape[0], -1)
     col_count = weight_local.shape[1]
-    weight_full = lax.all_gather(weight_local, ("dp", "ctx"), axis=0, tiled=True)
+    weight_full = jnp.concatenate(
+        lax.all_to_all(
+            jnp.stack([weight_local] * lax.axis_size(("dp", "ctx"))), ("dp", "ctx"), 0, 0
+        ),
+        axis=0,
+    )
     bc_sums = jnp.dot(tokens, weight_full, preferred_element_type=jnp.float32)
     group_count = col_count // (2 * STATE)
     head_count = values_in.shape[2] // HEAD_DIM

time: 1730 us -> 1670 us (0.965)
  waiting for transfers between devices: 1410 us -> 1340 us
    all_gather x1 -> x0, waiting for transfers between devices: 110 us -> none  [body(): lax.all_gather(weight_local, ('dp', 'ctx'), axis=0, tiled=True)]
    unnamed x6 -> x5, waiting for transfers between devices: 591 us -> 685 us
    all_gather x2, waiting for transfers between devices: 598 us -> 504 us  [carried_in(): gathered = jax.tree.map(lambda a: lax.all_gather(a, axis), part)]
    all_to_all x0 -> x1, waiting for transfers between devices: none -> 39.1 us  [body(): lax.all_to_all(jnp.stack([weight_local] * lax.axis_size(('dp', 'ctx'))),...]
  transfers between devices with their start and end apart: 5 -> 5, of which waited for: 5 -> 5; matrix products, arithmetic and copies ran while one was open for 2% -> 7% of each run, Pallas kernels for 0% -> 0%
where the time goes in v1:
time: 1670 us; the launch traced here: 1660 us
  waiting for transfers between devices  1340 us (80%)
  blocking collectives  144 us (9%)
  other arithmetic  91.3 us (5%)
  local copies, waits for them, and re-layouts  35.6 us (2%)
  matrix products  20.4 us (1%)
    unnamed x5, waiting for transfers between devices  685 us
    all_gather x2, waiting for transfers between devices, carried_in(): gathered = jax.tree.map(lambda a: lax.all_gather(a, axis), part)  504 us
    unnamed x1, blocking collectives  144 us
    reduce_scatter x1, waiting for transfers between devices, body(): lax.psum_scatter(input_terms.astype(jnp.bfloat16), 'head', scatter_dimens...  110 us
    add x63, other arithmetic, chain(): earlier[1] * jnp.repeat(later[0], HEAD_DIM)[None, :] + later[1]  79.2 us
    all_to_all x1, waiting for transfers between devices, body(): lax.all_to_all(jnp.stack([weight_local] * lax.axis_size(('dp', 'ctx'))),...  39.1 us
  transfers between devices with their start and end apart: 5, of which 5 were waited for; matrix products, arithmetic and copies ran while one was open for 7% of the time, Pallas kernels for 0%

profile of v1, /device:TPU:1, one launch (start us, length us, event | category | flops | bytes accessed | tf_op | source)
XLA Modules:
  0.0 1663.2 jit_solution(827760737881968302)
XLA Ops:
  9.6 16.3 all-to-all-start
  26.0 2.0 copy.44
  28.0 2.1 convert_element_type.116
  30.1 2.0 copy.45
  32.2 2.1 convert_element_type.117
  34.9 2.0 copy.46
  37.0 2.6 multiply_convert_fusion
  39.7 39.1 %all-to-all-done = bf16[128,32,256]{2,1,0:T(8,128)(2,1)S(1)} async-done(((bf16[128,32,256]{2,1,0:T(8,128)(2,1)}), bf16[128,32,256]{2,1,0:T(8,128)(2,1)S(1)}, u32[]{:S(2)}, u32[]{:S(2)}) %all-to-all-start) | async-done | bytes 2097184 | tf_op jit(solution)/shard_map/all_to_all | solution.py:129
  79.3 2.8 fusion.19
  83.6 1.7 fusion.16
  89.0 144.2 %all-reduce = f32[2048]{0:T(1024)S(1)} all-reduce(f32[2048]{0:T(1024)S(1)} %dynamic-update-slice), channel_id=2, replica_groups=mesh['dp'=2,'ctx'=64,'head'=2] {'ctx'}, use_global_device_ids=true, to_apply=%add | all-reduce | flops 2048 | bytes 16384
  233.2 225.4 %all-gather.4.cloned.1.call-done = f32[64,64,2048]{2,1,0:T(8,128)} async-done(((f32[1,64,2048]{2,1,0:T(8,128)}), f32[64,64,2048]{2,1,0:T(8,128)}) %all-gather.4.cloned.1.call-update) | async-done | bytes 33554448 | tf_op jit(solution)/shard_map/all_gather | solution.py:15
  458.6 90.8 %while.26 = (s32[]{:T(128)}, f32[64,2048]{1,0:T(8,128)S(1)}, s32[]{:T(128)}, f32[64,32]{1,0:T(8,128)S(1)}, f32[64,64,2048]{2,1,0:T(8,128)}, /*index=5*/s32[]{:T(128)}, s32[]{:T(128)}, s32[]{:T(128)}, s32[]{:T(128)}) while((s32[]{:T(128)}, f32[64,2048]{1,0:T(8,128)S(1)}, s32[]{:T(128)}, f32[64,32]{1,0:T(8,128)S(1)}, f32[64,64,2048]{2,1,0:T(8,128)}, ...), condition=%wide.region_3.4_spmd, body=%wide.region_2.3_spmd.sunk | while | flops 262150 | bytes 1606171 | solution.py:24
  549.8 1.9 convolution_bitcast_fusion.3
  553.2 278.8 %all-gather.6.cloned.1.call-done = f32[64,64,2048]{2,1,0:T(8,128)} async-done(((f32[1,64,2048]{2,1,0:T(8,128)}), f32[64,64,2048]{2,1,0:T(8,128)}) %all-gather.6.cloned.1.call-update) | async-done | bytes 33554448 | tf_op jit(solution)/shard_map/all_gather | solution.py:15
  833.1 1.9 convolution_bitcast_fusion.2
  835.0 3.0 bitcast_multiply_fusion.2
  839.4 2.7 fusion
  842.1 5.6 copy.61
  849.3 1.8 convolution_convert_fusion
  852.4 2.5 fusion.11
  854.9 2.0 copy.54
  860.5 684.5 %reduce-scatter.7.cloned.1.call-done = f32[32,256]{1,0:T(8,128)} async-done(((f32[4096,256]{1,0:T(8,128)}), f32[32,256]{1,0:T(8,128)}) %reduce-scatter.7.cloned.1.call-update) | async-done | bytes 32784
  1546.6 110.1 %reduce-scatter.5.cloned.1.call-done = bf16[128,2048]{1,0:T(8,128)(2,1)} async-done(((bf16[128,4096]{1,0:T(8,128)(2,1)}), bf16[128,2048]{1,0:T(8,128)(2,1)}) %reduce-scatter.5.cloned.1.call-update) | async-done | bytes 524304 | tf_op jit(solution)/shard_map/reduce_scatter | solution.py:206
  (330 shorter events, 109.5 us)
Async XLA Ops:
  7.2 71.5 %copy-start = (bf16[1,128,4096]{2,1,0:T(8,128)(2,1)S(1)}, bf16[1,128,4096]{2,1,0:T(8,128)(2,1)}, u32[]{:S(2)}) copy-start(bf16[1,128,4096]{2,1,0:T(8,128)(2,1)} %param.11) | copy-start | bytes 3145732
  9.6 69.1 %all-to-all-start = ((bf16[128,32,256]{2,1,0:T(8,128)(2,1)}), bf16[128,32,256]{2,1,0:T(8,128)(2,1)S(1)}, u32[]{:S(2)}, u32[]{:S(2)}) async-start(bf16[128,32,256]{2,1,0:T(8,128)(2,1)} %stack.15), calls=%async_computation | async-start | bytes 4194304 | tf_op jit(solution)/shard_map/all_to_all | solution.py:129
  25.9 432.7 %all-gather.4.cloned.1.call-start = ((), (), s32[]{:S(2)}) async-start(), calls=%async_computation.3 | async-start | bytes 34078720 | tf_op jit(solution)/shard_map/all_gather | solution.py:15
  28.0 6.3 copy-start.14
  78.7 3.4 copy-start.1
  85.3 2.2 copy-start.16
  86.8 745.3 %all-gather.6.cloned.1.call-start = ((), (), s32[]{:S(2)}) async-start(), calls=%async_computation.4 | async-start | bytes 34078720 | tf_op jit(solution)/shard_map/all_gather | solution.py:15
  87.5 1457.5 %reduce-scatter.7.cloned.1.call-start = ((), (), s32[]{:S(2)}) async-start(), calls=%async_computation.6 | async-start | bytes 4227072
  458.6 91.1 %copy-start.9 = (bf16[1,128,2048]{1,2,0:T(8,128)(2,1)S(1)}, bf16[1,128,2048]{1,2,0:T(8,128)(2,1)}, u32[]{:S(2)}) copy-start(bf16[1,128,2048]{1,2,0:T(8,128)(2,1)} %copy.46) | copy-start | bytes 1572868
  832.1 1.0 copy-start.8
  832.6 5.3 copy-start.3
  832.6 2.4 copy-start.5
  835.0 3.0 copy-start.10
  838.0 1.1 copy-start.13
  847.7 1.6 copy-start.2
  847.8 4.4 copy-start.15
  847.8 808.9 %reduce-scatter.5.cloned.1.call-start = ((), (), s32[]{:S(2)}) async-start(), calls=%async_computation.5 | async-start | bytes 1572864 | tf_op jit(solution)/shard_map/reduce_scatter | solution.py:206
  851.2 1.2 copy-start.12
  852.4 4.6 copy-start.4
  857.0 1.2 copy-start.6
  857.0 1.5 copy-start.7
  857.0 1.7 copy-start.11
Sparse Core Ops, SparseCore 0:
  86.9 371.6 all-gather.3
  460.4 371.6 all-gather.5
  847.9 697.0 reduce-scatter.6
  1547.9 108.7 reduce-scatter.4
